TPU v7x, 128 devices: a whole 4x4x4 slice. The times are simulated.
128 devices in a mesh: ens: 8 (over y, core), trc: 16 (over z, x).
Axes of the slice: x: 4, y: 4, z: 4, core: 2. Of those that a mesh axis runs over, the one named last changes fastest.
Arguments:
- tracer_state: bfloat16 [3072, 4, 16, 1440], P(('ens', 'trc')), may hold values from -6 to 6
- velocity: float32 [2, 4, 16, 1440], replicated, may hold values from -0.24 to 0.24
- land_mask: int32 [16, 1440], replicated, may hold values from 0 to 1, as said below
- in_weight: bfloat16 [24, 256], replicated, may hold values from -1.25 to 1.25
- bias_one: float32 [256], replicated, may hold values from -3 to 3
- hid_weight: bfloat16 [256, 256], replicated, may hold values from -0.375 to 0.375
- bias_two: float32 [256], replicated, may hold values from -3 to 3
- out_coef: float32 [128, 24, 256], P('ens'), may hold values from -6 to 6
- obs_cell: int32 [16, 128], P('trc'), may hold values from 0 to 5759, as said below
- obs_count: int32 [16], P('trc'), may hold values from 16 to 128, as said below
- obs_value: float32 [16, 6, 128], P('trc'), may hold values from -6 to 6
- obs_var: float32 [16, 6, 128], P('trc'), may hold values from 0.05 to 0.5
- obs_noise: float32 [128, 16, 6, 128], P(None, 'trc'), may hold values from -2 to 2
Outputs:
- new_state: bfloat16 [3072, 4, 16, 1440], P('ens', None, 'trc')
- new_coef: float32 [128, 24, 256], P('ens')
Inputs may be any that keep to these rules, and one draw needn't show every extreme that they name: `land_mask`: every block of 1 latitude rows (rows k * 1 to (k + 1) - 1) holds at most 1152 ocean columns, and some block exactly 1152. `obs_cell`: every slot names an ocean cell of its block. `obs_count`: some block uses all 128 slots.
All inputs are finite; a program needn't handle non-finite values.
Results may differ from a plain program's by a relative error of at most 0.0068.
Values may be sent and summed in bfloat16 or wider, within the bound.
No kernel may reach another device: no remote copies, remote signals or barrier semaphores. Data moves between devices by JAX's collectives and lax.ppermute only.
A program may use at most 128 MiB of HBM per device.

v0:
```python
import jax
import jax.numpy as jnp
from jax import lax
from jax.sharding import PartitionSpec as P

OBS_TR = 6
ADV_STEPS = 2
OBS_CAP = 128


def transport(concentration, velocity, sea_mask):
    east_open = sea_mask * jnp.roll(sea_mask, -1, axis=1)
    north_open = sea_mask * jnp.concatenate([sea_mask[1:], jnp.zeros_like(sea_mask[:1])], axis=0)
    east_speed = velocity[0] * east_open
    north_speed = velocity[1] * north_open
    for _ in range(ADV_STEPS):
        east_value = jnp.roll(concentration, -1, axis=-1)
        east_flux = (
            jnp.maximum(east_speed, 0.0) * concentration + jnp.minimum(east_speed, 0.0) * east_value
        )
        north_value = jnp.concatenate(
            [concentration[..., 1:, :], jnp.zeros_like(concentration[..., :1, :])], axis=-2
        )
        north_flux = (
            jnp.maximum(north_speed, 0.0) * concentration
            + jnp.minimum(north_speed, 0.0) * north_value
        )
        west_flux = jnp.roll(east_flux, 1, axis=-1)
        south_flux = jnp.concatenate(
            [jnp.zeros_like(north_flux[..., :1, :]), north_flux[..., :-1, :]], axis=-2
        )
        concentration = concentration - (east_flux - west_flux) - (north_flux - south_flux)
    return concentration


def reaction(fields, in_weight, bias_one, hid_weight, bias_two, member_coef, sea_cells):
    contract = (((0,), (0,)), ((), ()))
    hidden_one = lax.dot_general(in_weight, fields, contract, preferred_element_type=jnp.float32)
    hidden_one = jax.nn.silu(hidden_one + bias_one[:, None]).astype(jnp.bfloat16)
    hidden_two = lax.dot_general(
        hid_weight, hidden_one, contract, preferred_element_type=jnp.float32
    )
    hidden_two = jax.nn.silu(hidden_two + bias_two[:, None]).astype(jnp.bfloat16)
    tendency = jnp.dot(
        member_coef, hidden_two, preferred_element_type=jnp.float32
    ) * hid_weight.shape[0] ** (-0.5)
    return ((fields.astype(jnp.float32) + tendency) * sea_cells).astype(jnp.bfloat16)


def solve_system(system, right_side):
    factor = jnp.linalg.cholesky(system)
    middle = lax.linalg.triangular_solve(factor, right_side, left_side=True, lower=True)
    return lax.linalg.triangular_solve(factor, middle, left_side=True, lower=True, transpose_a=True)


def shards(
    tracer_state,
    velocity,
    land_mask,
    in_weight,
    bias_one,
    hid_weight,
    bias_two,
    out_coef,
    obs_cell,
    obs_count,
    obs_value,
    obs_var,
    obs_noise,
):
    blocks = lax.axis_size("trc")
    own_block = lax.axis_index("trc")
    group_index = lax.axis_index("ens")
    field_rows, levels, lat_rows, lon_count = tracer_state.shape
    row_block = lat_rows // blocks
    block_width = row_block * lon_count
    members_here = out_coef.shape[0]
    tracers = in_weight.shape[0]
    group_rows = members_here * tracers
    highest = lax.Precision.HIGHEST
    sea_mask = land_mask.astype(jnp.float32)
    advected = transport(tracer_state.astype(jnp.float32) * sea_mask, velocity, sea_mask).astype(
        jnp.bfloat16
    )
    coef_half = out_coef.astype(jnp.bfloat16)
    sea_own = lax.dynamic_slice_in_dim(sea_mask, own_block * row_block, row_block, 0)
    gathered = lax.all_to_all(advected, "trc", split_axis=2, concat_axis=0, tiled=True)
    out_shape = gathered.shape
    grouped = gathered.reshape(members_here, tracers, -1)
    sea_cells = jnp.broadcast_to(sea_own[None], (out_shape[1],) + sea_own.shape).reshape(-1)

    def one_member(inputs):
        fields, member_coef = inputs
        return reaction(fields, in_weight, bias_one, hid_weight, bias_two, member_coef, sea_cells)

    reacted = lax.map(one_member, (grouped, coef_half))
    new_cols = reacted.reshape(out_shape)
    new_flat = new_cols.reshape(group_rows, levels, block_width)
    observed = new_flat.reshape(members_here, tracers, levels * block_width)[:, :OBS_TR]
    cell_index = jnp.broadcast_to(obs_cell[0][None, None], (members_here, OBS_TR, OBS_CAP))
    predicted_own = jnp.take_along_axis(observed, cell_index, axis=2)
    predicted_all = lax.all_gather(predicted_own, "ens", axis=0, tiled=True)
    member_total = predicted_all.shape[0]
    slot_ids = jnp.arange(OBS_CAP, dtype=jnp.int32)
    valid_slots = (slot_ids < obs_count[0]).astype(jnp.float32)
    weight = valid_slots[None, :] / obs_var[0]
    guessed = predicted_all.astype(jnp.float32).reshape(member_total, -1)
    anomaly = guessed - jnp.mean(guessed, axis=0)
    misfit = (obs_value[None] + obs_noise).reshape(member_total, -1) - guessed
    weighted = anomaly * weight.reshape(1, -1)
    gram_part = jnp.dot(weighted, anomaly.T, precision=highest, preferred_element_type=jnp.float32)
    cross_part = jnp.dot(weighted, misfit.T, precision=highest, preferred_element_type=jnp.float32)
    gram, cross = lax.psum((gram_part, cross_part), "trc")
    system = (member_total - 1) * jnp.eye(member_total, dtype=jnp.float32) + gram
    mixing = solve_system(system, cross)
    flat_coef = out_coef.reshape(members_here, -1)
    first_member = group_index * members_here
    mixing_rows = lax.dynamic_slice_in_dim(mixing, first_member, members_here, 0)
    summed = lax.psum_scatter(
        jnp.dot(mixing_rows.T, flat_coef, precision=highest, preferred_element_type=jnp.float32),
        "ens",
        scatter_dimension=0,
        tiled=True,
    )
    new_coef = flat_coef + summed
    return (new_cols, new_coef.reshape(members_here, tracers, -1))


def solution(mesh):
    in_specs = (
        P(("ens", "trc"), None, None, None),
        P(),
        P(),
        P(),
        P(),
        P(),
        P(),
        P("ens", None, None),
        P("trc", None),
        P("trc"),
        P("trc", None, None),
        P("trc", None, None),
        P(None, "trc", None, None),
    )
    out_specs = (P("ens", None, "trc", None), P("ens", None, None))
    return jax.shard_map(shards, mesh=mesh, in_specs=in_specs, out_specs=out_specs, check_vma=False)
```

profile of v0, /device:TPU:0, one launch (start us, length us, event | category | flops | bytes accessed | tf_op | source)
XLA Modules:
  0.0 646.9 jit_solution(13384533224822212277)
XLA Ops:
  8.2 5.3 convert_multiply_fusion
  13.4 6.1 slice.97
  26.1 13.3 %multiply_add_fusion.1 = (f32[24,4,16,1440]{3,0,1,2:T(8,128)S(1)}, f32[24,4,16,1440]{3,0,1,2:T(8,128)S(1)}) fusion(f32[24,4,15,1440]{3,0,1,2:T(8,128)} %slice.102, f32[4,16,1440]{2,0,1:T(4,128)S(1)} %copy.69, f32[4,16,1440]{2,0,1:T(4,128)S(1)} %copy.68, f32[16,1440]{1,0:T(8,128)S(1)} %convert_element_type.36, bf16[24,4,16,1440]{3,2,1,0:T(8,128)(2,1)} %param.15, ...), kind=kLoop, calls=%fused_computation.34 | loop fusion | flops 19906560 | bytes 40826880 | tf_op jit(solution)/shard_map/add | solution.py:25
  39.4 4.7 slice.103
  48.7 15.4 %fusion.18 = f32[24,4,16,1440]{3,0,1,2:T(8,128)S(1)} fusion(f32[24,4,16,1440]{3,0,1,2:T(8,128)} %copy-done, f32[24,4,16,1439]{3,0,1,2:T(8,128)} %bitcast.96, f32[24,4,16,1]{3,0,1,2:T(8,128)} %slice.99, f32[24,4,16,1440]{3,0,1,2:T(8,128)} %copy-done.1, f32[24,4,15,1440]{3,0,1,2:T(8,128)} %slice.103, f32[16,1440]{1,0:T(8,128)S(1)} %convert_element_type.36, ...), kind=kLoop, calls=%fused_computation.26 | loop fusion | flops 15482880 | bytes 48199680 | tf_op jit(solution)/shard_map/sub | solution.py:32
  64.1 6.2 slice.104
  74.6 17.6 %multiply_add_fusion = (f32[24,4,16,1440]{3,0,1,2:T(8,128)}, f32[24,4,16,1440]{3,0,1,2:T(8,128)}) fusion(f32[24,4,15,1440]{3,0,1,2:T(8,128)} %slice.108, f32[24,4,16,1440]{3,0,1,2:T(8,128)S(1)} %fusion.18, f32[4,16,1440]{2,0,1:T(4,128)S(1)} %copy.69, f32[4,16,1440]{2,0,1:T(4,128)S(1)} %copy.68, f32[24,4,16,1]{3,0,1,2:T(8,128)S(1)} %slice.105, ...), kind=kLoop, calls=%fused_computation.33 | loop fusion | flops 15482880 | bytes 45158400 | tf_op jit(solution)/shard_map/add | solution.py:25
  92.2 8.2 %slice.109 = f32[24,4,15,1440]{3,0,1,2:T(8,128)} slice(f32[24,4,16,1440]{3,0,1,2:T(8,128)} %get-tuple-element.101), slice={[0:24], [0:4], [0:15], [0:1440]} | slice | bytes 16588800 | tf_op jit(solution)/shard_map/slice | solution.py:30
  101.8 16.0 %fusion.22 = bf16[24,4,16,1440]{3,0,1,2:T(8,128)(2,1)} fusion(f32[24,4,16,1440]{3,0,1,2:T(8,128)S(1)} %fusion.18, f32[24,4,16,1440]{3,0,1,2:T(8,128)} %get-tuple-element.102, f32[24,4,16,1439]{3,0,1,2:T(8,128)} %bitcast.95, f32[24,4,16,1]{3,0,1,2:T(8,128)S(1)} %slice.106, f32[24,4,16,1440]{3,0,1,2:T(8,128)} %get-tuple-element.101, f32[24,4,15,1440]{3,0,1,2:T(8,128)} %slice.109), kind=kLoop, calls=%fused_computation.32 | loop fusion | flops 13271040 | bytes 48107520 | tf_op jit(solution)/shard_map/convert_element_type | solution.py:82
  117.8 8.2 %all-to-all-start = ((bf16[24,4,16,1440]{3,0,1,2:T(8,128)(2,1)}), bf16[24,4,16,1440]{3,0,1,2:T(8,128)(2,1)}, u32[]{:S(2)}, u32[]{:S(2)}) async-start(bf16[24,4,16,1440]{3,0,1,2:T(8,128)(2,1)} %fusion.22), calls=%async_computation | async-start | bytes 9437184 | tf_op jit(solution)/shard_map/all_to_all | solution.py:87
  126.9 69.9 %all-to-all-done = bf16[24,4,16,1440]{3,0,1,2:T(8,128)(2,1)} async-done(((bf16[24,4,16,1440]{3,0,1,2:T(8,128)(2,1)}), bf16[24,4,16,1440]{3,0,1,2:T(8,128)(2,1)}, u32[]{:S(2)}, u32[]{:S(2)}) %all-to-all-start) | async-done | bytes 4423712 | tf_op jit(solution)/shard_map/all_to_all | solution.py:87
  196.8 7.0 %copy.70 = bf16[16,24,4,1,1440]{4,2,1,0,3:T(4,128)(2,1)} copy(bf16[16,24,4,1,1440]{4,1,2,0,3:T(8,128)(2,1)} %bitcast.5) | data formatting | bytes 8847360 | tf_op jit(solution)/shard_map/all_to_all | solution.py:87
  203.8 8.6 %reshape.106 = bf16[16,24,5760]{2,1,0:T(8,128)(2,1)} reshape(bf16[16,24,4,1,1440]{4,2,1,0,3:T(4,128)(2,1)} %copy.70) | data formatting | bytes 8847360 | tf_op jit(solution)/shard_map/reshape | solution.py:89
  212.5 141.6 %while.11 = (s32[]{:T(128)}, bf16[16,24,5760]{2,1,0:T(8,128)(2,1)}, bf16[16,24,5760]{2,1,0:T(8,128)(2,1)}, bf16[16,24,256]{2,1,0:T(8,128)(2,1)S(1)}, bf16[24,256...) while((s32[]{:T(128)}, bf16[16,24,5760]{2,1,0:T(8,128)(2,1)}, ...), condition=%wide.region_1.2_spmd.clone, body=%wide.region_0.1_spmd.clone.sunk | while | flops 914918400 | bytes 6986469 | solution.py:96
  216.9 4.4 fusion.57
  225.8 4.4 fusion.57
  234.6 4.4 fusion.57
  243.5 4.4 fusion.57
  252.3 4.4 fusion.57
  261.2 4.4 fusion.57
  270.0 4.4 fusion.57
  278.9 4.4 fusion.57
  287.7 4.4 fusion.57
  296.6 4.4 fusion.57
  355.6 116.4 %gather_fusion = bf16[12288]{0:T(1024)(128)(2,1)S(1)} fusion(bf16[16,6,5760]{2,1,0:T(8,128)(2,1)S(1)} %slice.91, s32[12288]{0:T(1024)S(1)} %reshape.111), kind=kCustom, calls=%fused_computation | custom fusion | bytes 196608 | tf_op jit(solution)/shard_map/jit(take_along_axis)/gather | solution.py:101
  472.1 13.5 %all_gather.3 = bf16[128,6,128]{2,0,1:T(8,128)(2,1)S(1)} all-gather(bf16[16,6,128]{2,0,1:T(8,128)(2,1)S(1)} %copy.71), channel_id=1, replica_groups=mesh['ens'=8,'trc'=16] {'ens'}, dimensions={0}, use_global_device_ids=true | all-gather | bytes 221184 | tf_op jit(solution)/shard_map/all_gather | solution.py:102
  490.0 82.2 %all-reduce.8.cloned.1.call-done = (f32[128,128]{1,0:T(8,128)}, f32[128,128]{1,0:T(8,128)}) async-done(((f32[128,128]{1,0:T(8,128)}, f32[128,128]{1,0:T(8,128)}), (f32[128,128]{1,0:T(8,128)}, f32[128,128]{1,0:T(8,128)})) %all-reduce.8.cloned.1.call-update) | async-done | bytes 131088 | tf_op jit(solution)/shard_map/psum | solution.py:113
  574.0 11.7 %cholesky.16 = f32[128,128]{1,0:T(8,128)S(1)} custom-call(f32[128,128]{1,0:T(8,128)S(1)} %fusion.31), custom_call_target="Cholesky" | custom-call | tf_op jit(solution)/shard_map/jit(cholesky)/cholesky | solution.py:51
  587.1 9.8 %custom-call.8 = f32[1,128,128]{1,2,0:T(8,128)S(1)} custom-call(f32[1,128,128]{2,1,0:T(8,128)S(1)} %fusion.26), custom_call_target="InvertDiagBlocksLowerTriangular" | custom-call | tf_op jit(solution)/shard_map/triangular_solve | solution.py:53
  602.5 10.5 %reshape.107 = bf16[384,4,1,1440]{3,1,0,2:T(4,128)(2,1)} reshape(bf16[16,24,5760]{2,1,0:T(8,128)(2,1)} %get-tuple-element.49) | data formatting | bytes 8847360 | tf_op jit(solution)/shard_map/reshape | solution.py:97
  613.1 8.9 %copy.79 = bf16[384,4,1,1440]{0,3,2,1:T(8,128)(2,1)} copy(bf16[384,4,1,1440]{3,1,0,2:T(4,128)(2,1)} %reshape.107) | data formatting | bytes 8847360
  621.9 16.0 %reduce-scatter.2.cloned.1.call-done = f32[16,6144]{1,0:T(8,128)} async-done(((f32[128,6144]{1,0:T(8,128)}), f32[16,6144]{1,0:T(8,128)}) %reduce-scatter.2.cloned.1.call-update) | async-done | bytes 393232 | tf_op jit(solution)/shard_map/reduce_scatter | solution.py:119
  (135 shorter events, 132.2 us)
Async XLA Ops:
  19.6 5.2 copy-start.5
  19.6 5.3 copy-start.3
  39.4 6.5 %copy-start = (f32[24,4,16,1440]{3,0,1,2:T(8,128)}, f32[24,4,16,1440]{3,0,1,2:T(8,128)S(1)}, u32[]{:S(2)}) copy-start(f32[24,4,16,1440]{3,0,1,2:T(8,128)S(1)} %get-tuple-element.104) | copy-start | bytes 26542084
  39.4 9.3 %copy-start.1 = (f32[24,4,16,1440]{3,0,1,2:T(8,128)}, f32[24,4,16,1440]{3,0,1,2:T(8,128)S(1)}, u32[]{:S(2)}) copy-start(f32[24,4,16,1440]{3,0,1,2:T(8,128)S(1)} %get-tuple-element.103) | copy-start | bytes 26542084
  117.8 8.3 %copy-start.2 = (f32[16,24,256]{2,1,0:T(8,128)S(1)}, f32[16,24,256]{2,1,0:T(8,128)}, u32[]{:S(2)}) copy-start(f32[16,24,256]{2,1,0:T(8,128)} %param.22) | copy-start | bytes 1179652
  117.8 8.3 %copy-start.8 = (s32[1,128]{1,0:T(1,128)S(1)}, s32[1,128]{1,0:T(1,128)}, u32[]{:S(2)}) copy-start(s32[1,128]{1,0:T(1,128)} %param.23) | copy-start | bytes 1540
  117.8 9.0 %copy-start.6 = (f32[1,6,128]{2,0,1:T(1,128)S(1)}, f32[1,6,128]{2,0,1:T(1,128)}, u32[]{:S(2)}) copy-start(f32[1,6,128]{2,0,1:T(1,128)} %param.25) | copy-start | bytes 9220
  117.8 9.1 %copy-start.7 = (f32[1,6,128]{2,0,1:T(1,128)S(1)}, f32[1,6,128]{2,0,1:T(1,128)}, u32[]{:S(2)}) copy-start(f32[1,6,128]{2,0,1:T(1,128)} %param.26) | copy-start | bytes 9220
  117.8 79.0 %all-to-all-start = ((bf16[24,4,16,1440]{3,0,1,2:T(8,128)(2,1)}), bf16[24,4,16,1440]{3,0,1,2:T(8,128)(2,1)}, u32[]{:S(2)}, u32[]{:S(2)}) async-start(bf16[24,4,16,1440]{3,0,1,2:T(8,128)(2,1)} %fusion.22), calls=%async_computation | async-start | bytes 9437184 | tf_op jit(solution)/shard_map/all_to_all | solution.py:87
  126.0 446.2 %all-reduce.8.cloned.1.call-start = ((), (), s32[]{:S(2)}) async-start(), calls=%async_computation.3 | async-start | bytes 262144 | tf_op jit(solution)/shard_map/psum | solution.py:113
  196.8 15.6 %copy-start.9 = (bf16[256,256]{1,0:T(8,128)(2,1)S(1)}, bf16[256,256]{1,0:T(8,128)(2,1)}, u32[]{:S(2)}) copy-start(bf16[256,256]{1,0:T(8,128)(2,1)} %param.20) | copy-start | bytes 393220
  196.8 15.6 %copy-start.10 = (bf16[24,256]{1,0:T(8,128)(2,1)S(1)}, bf16[24,256]{1,0:T(8,128)(2,1)}, u32[]{:S(2)}) copy-start(bf16[24,256]{1,0:T(8,128)(2,1)} %param.18) | copy-start | bytes 36868
  196.8 15.6 %copy-start.11 = (f32[256]{0:T(256)S(1)}, f32[256]{0:T(256)}, u32[]{:S(2)}) copy-start(f32[256]{0:T(256)} %param.19) | copy-start | bytes 3076
  196.8 15.6 %copy-start.12 = (f32[256]{0:T(256)S(1)}, f32[256]{0:T(256)}, u32[]{:S(2)}) copy-start(f32[256]{0:T(256)} %param.21) | copy-start | bytes 3076
  355.6 132.6 %copy-start.4 = (f32[128,1,6,128]{3,1,2,0:T(1,128)S(1)}, f32[128,1,6,128]{3,1,2,0:T(1,128)}, u32[]{:S(2)}) copy-start(f32[128,1,6,128]{3,1,2,0:T(1,128)} %param.27) | copy-start | bytes 1179652
  489.8 148.1 %reduce-scatter.2.cloned.1.call-start = ((), (), s32[]{:S(2)}) async-start(), calls=%async_computation.2 | async-start | bytes 3538944 | tf_op jit(solution)/shard_map/reduce_scatter | solution.py:119
Sparse Core Ops, SparseCore 0:
  490.0 82.1 all-reduce.7
  602.7 35.2 reduce-scatter.1
where the time goes:
time: 654 us; the launch traced here: 647 us
  local copies, waits for them, and re-layouts  198 us (30%)
  waiting for transfers between devices  168 us (26%)
  matrix products  148 us (23%)
  other arithmetic  94.8 us (14%)
  between operations  15.3 us (2%)
  blocking collectives  13.5 us (2%)
  starting transfers between devices  8.26 us (1%)
    gather x3, local copies, waits for them, and re-layouts, shards(): predicted_own = jnp.take_along_axis(observed, cell_index, axis=2)  116 us
    psum x1, waiting for transfers between devices, shards(): gram, cross = lax.psum((gram_part, cross_part), 'trc')  82.2 us
    dot_general x16, matrix products, reaction(): jnp.dot(member_coef, hidden_two, preferred_element_type=jnp.float32)  70.3 us
    all_to_all x1, waiting for transfers between devices, shards(): lax.all_to_all(advected, 'trc', split_axis=2, concat_axis=0, tiled=True)  69.9 us
    dot_general x16, matrix products, reaction(): lax.dot_general(in_weight, fields, contract, preferred_element_type=jnp.f...  69.3 us
    add x2, other arithmetic, transport(): jnp.maximum(north_speed, 0.0) * concentration  30.8 us
    reduce_scatter x1, waiting for transfers between devices, shards(): lax.psum_scatter(jnp.dot(mixing_rows.T, flat_coef, precision=highest, pre...  16 us
    convert_element_type x1, other arithmetic, shards(): transport(tracer_state.astype(jnp.float32) * sea_mask, velocity, sea_mask)  16 us
  transfers between devices with their start and end apart: 3, of which 3 were waited for; matrix products, arithmetic and copies ran while one was open for 3% of the time, Pallas kernels for 0%

commit v1 on v0

--- a/solution.py
+++ b/solution.py
@@ -33,14 +33,29 @@
     return concentration
 
 
+def silu(value):
+    return value * (0.5 + 0.5 * jnp.tanh(0.5 * value))
+
+
+def tree_sum(value, axis_name, size):
+    if size & (size - 1):
+        return lax.psum(value, axis_name)
+    step = 1
+    while step < size:
+        pairs = [(i, i ^ step) for i in range(size)]
+        value = value + lax.ppermute(value, axis_name, pairs)
+        step *= 2
+    return value
+
+
 def reaction(fields, in_weight, bias_one, hid_weight, bias_two, member_coef, sea_cells):
     contract = (((0,), (0,)), ((), ()))
     hidden_one = lax.dot_general(in_weight, fields, contract, preferred_element_type=jnp.float32)
-    hidden_one = jax.nn.silu(hidden_one + bias_one[:, None]).astype(jnp.bfloat16)
+    hidden_one = silu(hidden_one + bias_one[:, None]).astype(jnp.bfloat16)
     hidden_two = lax.dot_general(
         hid_weight, hidden_one, contract, preferred_element_type=jnp.float32
     )
-    hidden_two = jax.nn.silu(hidden_two + bias_two[:, None]).astype(jnp.bfloat16)
+    hidden_two = silu(hidden_two + bias_two[:, None]).astype(jnp.bfloat16)
     tendency = jnp.dot(
         member_coef, hidden_two, preferred_element_type=jnp.float32
     ) * hid_weight.shape[0] ** (-0.5)
@@ -79,6 +94,7 @@
     group_rows = members_here * tracers
     highest = lax.Precision.HIGHEST
     sea_mask = land_mask.astype(jnp.float32)
+    coef_all = lax.all_gather(out_coef.reshape(out_coef.shape[0], -1), "ens", axis=0, tiled=True)
     advected = transport(tracer_state.astype(jnp.float32) * sea_mask, velocity, sea_mask).astype(
         jnp.bfloat16
     )
@@ -97,8 +113,11 @@
     new_cols = reacted.reshape(out_shape)
     new_flat = new_cols.reshape(group_rows, levels, block_width)
     observed = new_flat.reshape(members_here, tracers, levels * block_width)[:, :OBS_TR]
-    cell_index = jnp.broadcast_to(obs_cell[0][None, None], (members_here, OBS_TR, OBS_CAP))
-    predicted_own = jnp.take_along_axis(observed, cell_index, axis=2)
+    observed = observed.reshape(members_here * OBS_TR, levels * block_width)
+    cell_ids = lax.broadcasted_iota(jnp.int32, (levels * block_width, OBS_CAP), 0)
+    picker = (cell_ids == obs_cell[0][None, :]).astype(jnp.bfloat16)
+    picked = jnp.dot(observed, picker, preferred_element_type=jnp.float32)
+    predicted_own = picked.astype(jnp.bfloat16).reshape(members_here, OBS_TR, OBS_CAP)
     predicted_all = lax.all_gather(predicted_own, "ens", axis=0, tiled=True)
     member_total = predicted_all.shape[0]
     slot_ids = jnp.arange(OBS_CAP, dtype=jnp.int32)
@@ -110,18 +129,14 @@
     weighted = anomaly * weight.reshape(1, -1)
     gram_part = jnp.dot(weighted, anomaly.T, precision=highest, preferred_element_type=jnp.float32)
     cross_part = jnp.dot(weighted, misfit.T, precision=highest, preferred_element_type=jnp.float32)
-    gram, cross = lax.psum((gram_part, cross_part), "trc")
+    both = tree_sum(jnp.stack([gram_part, cross_part]), "trc", blocks)
+    gram, cross = both[0], both[1]
     system = (member_total - 1) * jnp.eye(member_total, dtype=jnp.float32) + gram
     mixing = solve_system(system, cross)
     flat_coef = out_coef.reshape(members_here, -1)
     first_member = group_index * members_here
-    mixing_rows = lax.dynamic_slice_in_dim(mixing, first_member, members_here, 0)
-    summed = lax.psum_scatter(
-        jnp.dot(mixing_rows.T, flat_coef, precision=highest, preferred_element_type=jnp.float32),
-        "ens",
-        scatter_dimension=0,
-        tiled=True,
-    )
+    mixing_cols = lax.dynamic_slice_in_dim(mixing, first_member, members_here, 1)
+    summed = jnp.dot(mixing_cols.T, coef_all, precision=highest, preferred_element_type=jnp.float32)
     new_coef = flat_coef + summed
     return (new_cols, new_coef.reshape(members_here, tracers, -1))
 

time: 654 us -> 452 us (0.69)
  local copies, waits for them, and re-layouts: 198 us -> 83.2 us
  waiting for transfers between devices: 168 us -> 84.8 us
    gather x3 -> x0, local copies, waits for them, and re-layouts: 116 us -> none  [shards(): predicted_own = jnp.take_along_axis(observed, cell_index, axis=2)]
    psum x1 -> x0, waiting for transfers between devices: 82.2 us -> none  [shards(): gram, cross = lax.psum((gram_part, cross_part), 'trc')]
    reduce_scatter x1 -> x0, waiting for transfers between devices: 16 us -> none  [shards(): lax.psum_scatter(jnp.dot(mixing_rows.T, flat_coef, precision=highest, pre...]
    ppermute x0 -> x4, waiting for transfers between devices: none -> 15.8 us  [tree_sum(): value = value + lax.ppermute(value, axis_name, pairs)]
  transfers between devices with their start and end apart: 3 -> 6, of which waited for: 3 -> 4; matrix products, arithmetic and copies ran while one was open for 3% -> 46% of each run, Pallas kernels for 0% -> 0%
where the time goes in v1:
time: 452 us; the launch traced here: 444 us
  matrix products  144 us (32%)
  other arithmetic  92 us (20%)
  waiting for transfers between devices  84.8 us (19%)
  local copies, waits for them, and re-layouts  83.2 us (18%)
  between operations  15.4 us (3%)
  blocking collectives  13.6 us (3%)
  starting transfers between devices  11.3 us (2%)
    dot_general x16, matrix products, reaction(): jnp.dot(member_coef, hidden_two, preferred_element_type=jnp.float32)  70 us
    all_to_all x1, waiting for transfers between devices, shards(): lax.all_to_all(advected, 'trc', split_axis=2, concat_axis=0, tiled=True)  68.9 us
    dot_general x16, matrix products, reaction(): lax.dot_general(in_weight, fields, contract, preferred_element_type=jnp.f...  66.8 us
    add x2, other arithmetic, transport(): jnp.maximum(north_speed, 0.0) * concentration  30.8 us
    convert_element_type x1, other arithmetic, shards(): transport(tracer_state.astype(jnp.float32) * sea_mask, velocity, sea_mask)  16.1 us
    ppermute x4, waiting for transfers between devices, tree_sum(): value = value + lax.ppermute(value, axis_name, pairs)  15.8 us
    sub x1, other arithmetic, transport(): concentration - (east_flux - west_flux) - (north_flux - south_flux)  15.4 us
    all_gather x1, blocking collectives, shards(): predicted_all = lax.all_gather(predicted_own, 'ens', axis=0, tiled=True)  13.6 us
  transfers between devices with their start and end apart: 6, of which 4 were waited for; matrix products, arithmetic and copies ran while one was open for 46% of the time, Pallas kernels for 0%

profile of v1, /device:TPU:0, one launch (start us, length us, event | category | flops | bytes accessed | tf_op | source)
XLA Modules:
  0.0 444.0 jit_solution(4422173835736729489)
XLA Ops:
  8.2 5.3 %convert_multiply_fusion = f32[24,4,16,1440]{3,0,1,2:T(8,128)S(1)} fusion(f32[16,1440]{1,0:T(8,128)S(1)} %convert_element_type.40, bf16[24,4,16,1440]{3,2,1,0:T(8,128)(2,1)} %param.15), kind=kLoop, calls=%fused_computation.34 | loop fusion | flops 4423680 | bytes 13363200 | tf_op jit(solution)/shard_map/mul | solution.py:98
  13.4 6.1 %slice.102 = f32[24,4,16,1439]{3,0,1,2:T(8,128)} slice(f32[24,4,16,1440]{3,0,1,2:T(8,128)S(1)} %convert_multiply_fusion), slice={[0:24], [0:4], [0:16], [1:1440]} | slice | bytes 17682432 | tf_op jit(solution)/shard_map/jit(_roll_static)/slice | solution.py:17
  26.1 13.0 %multiply_add_fusion.1 = (f32[24,4,16,1440]{3,0,1,2:T(8,128)S(1)}, f32[24,4,16,1440]{3,0,1,2:T(8,128)S(1)}) fusion(f32[24,4,15,1440]{3,0,1,2:T(8,128)} %slice.107, f32[4,16,1440]{2,0,1:T(4,128)S(1)} %copy.69, f32[4,16,1440]{2,0,1:T(4,128)S(1)} %copy.68, f32[16,1440]{1,0:T(8,128)S(1)} %convert_element_type.40, bf16[24,4,16,1440]{3,2,1,0:T(8,128)(2,1)} %param.15, ...), kind=kLoop, calls=%fused_computation.33 | loop fusion | flops 19906560 | bytes 40826880 | tf_op jit(solution)/shard_map/add | solution.py:25
  39.1 4.8 %slice.108 = f32[24,4,15,1440]{3,0,1,2:T(8,128)} slice(f32[24,4,16,1440]{3,0,1,2:T(8,128)S(1)} %get-tuple-element.101), slice={[0:24], [0:4], [0:15], [0:1440]} | slice | bytes 16588800 | tf_op jit(solution)/shard_map/slice | solution.py:30
  48.4 15.4 %fusion.18 = f32[24,4,16,1440]{3,0,1,2:T(8,128)S(1)} fusion(f32[24,4,16,1440]{3,0,1,2:T(8,128)} %copy-done, f32[24,4,16,1439]{3,0,1,2:T(8,128)} %bitcast.104, f32[24,4,16,1]{3,0,1,2:T(8,128)} %slice.104, f32[24,4,16,1440]{3,0,1,2:T(8,128)} %copy-done.1, f32[24,4,15,1440]{3,0,1,2:T(8,128)} %slice.108, f32[16,1440]{1,0:T(8,128)S(1)} %convert_element_type.40, ...), kind=kLoop, calls=%fused_computation.25 | loop fusion | flops 15482880 | bytes 48199680 | tf_op jit(solution)/shard_map/sub | solution.py:32
  63.8 6.2 %slice.109 = f32[24,4,16,1439]{3,0,1,2:T(8,128)} slice(f32[24,4,16,1440]{3,0,1,2:T(8,128)S(1)} %fusion.18), slice={[0:24], [0:4], [0:16], [1:1440]} | slice | bytes 17682432 | tf_op jit(solution)/shard_map/jit(_roll_static)/slice | solution.py:17
  74.4 17.8 %multiply_add_fusion = (f32[24,4,16,1440]{3,0,1,2:T(8,128)}, f32[24,4,16,1440]{3,0,1,2:T(8,128)}) fusion(f32[24,4,15,1440]{3,0,1,2:T(8,128)} %slice.113, f32[24,4,16,1440]{3,0,1,2:T(8,128)S(1)} %fusion.18, f32[4,16,1440]{2,0,1:T(4,128)S(1)} %copy.69, f32[4,16,1440]{2,0,1:T(4,128)S(1)} %copy.68, f32[24,4,16,1]{3,0,1,2:T(8,128)S(1)} %slice.110, ...), kind=kLoop, calls=%fused_computation.32 | loop fusion | flops 15482880 | bytes 45158400 | tf_op jit(solution)/shard_map/add | solution.py:25
  92.2 8.2 %slice.114 = f32[24,4,15,1440]{3,0,1,2:T(8,128)} slice(f32[24,4,16,1440]{3,0,1,2:T(8,128)} %get-tuple-element.99), slice={[0:24], [0:4], [0:15], [0:1440]} | slice | bytes 16588800 | tf_op jit(solution)/shard_map/slice | solution.py:30
  101.8 16.1 %fusion.22 = bf16[24,4,16,1440]{3,0,1,2:T(8,128)(2,1)} fusion(f32[24,4,16,1440]{3,0,1,2:T(8,128)S(1)} %fusion.18, f32[24,4,16,1440]{3,0,1,2:T(8,128)} %get-tuple-element.100, f32[24,4,16,1439]{3,0,1,2:T(8,128)} %bitcast.103, f32[24,4,16,1]{3,0,1,2:T(8,128)S(1)} %slice.111, f32[24,4,16,1440]{3,0,1,2:T(8,128)} %get-tuple-element.99, f32[24,4,15,1440]{3,0,1,2:T(8,128)} %slice.114), kind=kLoop, calls=%fused_computation.31 | loop fusion | flops 13271040 | bytes 48107520 | tf_op jit(solution)/shard_map/convert_element_type | solution.py:98
  117.9 8.2 %all-to-all-start = ((bf16[24,4,16,1440]{3,0,1,2:T(8,128)(2,1)}), bf16[24,4,16,1440]{3,0,1,2:T(8,128)(2,1)}, u32[]{:S(2)}, u32[]{:S(2)}) async-start(bf16[24,4,16,1440]{3,0,1,2:T(8,128)(2,1)} %fusion.22), calls=%async_computation | async-start | bytes 9437184 | tf_op jit(solution)/shard_map/all_to_all | solution.py:103
  128.0 68.9 %all-to-all-done = bf16[24,4,16,1440]{3,0,1,2:T(8,128)(2,1)} async-done(((bf16[24,4,16,1440]{3,0,1,2:T(8,128)(2,1)}), bf16[24,4,16,1440]{3,0,1,2:T(8,128)(2,1)}, u32[]{:S(2)}, u32[]{:S(2)}) %all-to-all-start) | async-done | bytes 4423712 | tf_op jit(solution)/shard_map/all_to_all | solution.py:103
  196.9 7.0 %copy.70 = bf16[16,24,4,1,1440]{4,2,1,0,3:T(4,128)(2,1)} copy(bf16[16,24,4,1,1440]{4,1,2,0,3:T(8,128)(2,1)} %bitcast.5) | data formatting | bytes 8847360 | tf_op jit(solution)/shard_map/all_to_all | solution.py:103
  203.9 8.6 %reshape.103 = bf16[16,24,5760]{2,1,0:T(8,128)(2,1)} reshape(bf16[16,24,4,1,1440]{4,2,1,0,3:T(4,128)(2,1)} %copy.70) | data formatting | bytes 8847360 | tf_op jit(solution)/shard_map/reshape | solution.py:105
  212.5 138.8 %while.11 = (s32[]{:T(128)}, bf16[16,24,5760]{2,1,0:T(8,128)(2,1)}, bf16[16,24,5760]{2,1,0:T(8,128)(2,1)}, bf16[16,24,256]{2,1,0:T(8,128)(2,1)S(1)}, bf16[24,256...) while((s32[]{:T(128)}, bf16[16,24,5760]{2,1,0:T(8,128)(2,1)}, ...), condition=%wide.region_1.2_spmd.clone, body=%wide.region_0.1_spmd.clone.sunk | while | flops 914918400 | bytes 6986469 | solution.py:112
  216.9 4.4 fusion.59
  234.2 4.4 fusion.59
  242.9 4.4 fusion.59
  251.6 4.4 fusion.59
  268.9 4.4 fusion.59
  277.6 4.4 fusion.59
  286.3 4.4 fusion.59
  294.9 4.4 fusion.59
  312.3 4.4 fusion.59
  321.0 4.4 fusion.59
  354.2 13.6 %all_gather.6 = bf16[128,6,128]{2,0,1:T(8,128)(2,1)S(1)} all-gather(bf16[16,6,128]{2,0,1:T(8,128)(2,1)S(1)} %copy.71), channel_id=1, replica_groups=mesh['ens'=8,'trc'=16] {'ens'}, dimensions={0}, use_global_device_ids=true | all-gather | bytes 221184 | tf_op jit(solution)/shard_map/all_gather | solution.py:121
  370.8 5.7 %collective-permute-done = f32[2,128,128]{2,1,0:T(8,128)S(1)} collective-permute-done((f32[2,128,128]{2,1,0:T(8,128)S(1)}, f32[2,128,128]{2,1,0:T(8,128)S(1)}, u32[]{:S(2)}, u32[]{:S(2)}) %collective-permute-start) | collective-permute-done | bytes 131104 | tf_op jit(solution)/shard_map/ppermute | solution.py:46
  377.5 5.6 %collective-permute-done.1 = f32[2,128,128]{2,1,0:T(8,128)S(1)} collective-permute-done((f32[2,128,128]{2,1,0:T(8,128)S(1)}, f32[2,128,128]{2,1,0:T(8,128)S(1)}, u32[]{:S(2)}, u32[]{:S(2)}) %collective-permute-start.1) | collective-permute-done | bytes 131104 | tf_op jit(solution)/shard_map/ppermute | solution.py:46
  383.7 4.5 %collective-permute-done.2 = f32[2,128,128]{2,1,0:T(8,128)S(1)} collective-permute-done((f32[2,128,128]{2,1,0:T(8,128)S(1)}, f32[2,128,128]{2,1,0:T(8,128)S(1)}, u32[]{:S(2)}, u32[]{:S(2)}) %collective-permute-start.2) | collective-permute-done | bytes 131104 | tf_op jit(solution)/shard_map/ppermute | solution.py:46
  389.7 10.5 %reshape.104 = bf16[384,4,1,1440]{3,1,0,2:T(4,128)(2,1)} reshape(bf16[16,24,5760]{2,1,0:T(8,128)(2,1)} %get-tuple-element.49) | data formatting | bytes 8847360 | tf_op jit(solution)/shard_map/reshape | solution.py:113
  400.2 8.8 %copy.79 = bf16[384,4,1,1440]{0,3,2,1:T(8,128)(2,1)} copy(bf16[384,4,1,1440]{3,1,0,2:T(4,128)(2,1)} %reshape.104) | data formatting | bytes 8847360
  409.2 11.7 %cholesky.16 = f32[128,128]{1,0:T(8,128)S(1)} custom-call(f32[128,128]{1,0:T(8,128)S(1)} %fusion.35), custom_call_target="Cholesky" | custom-call | tf_op jit(solution)/shard_map/jit(cholesky)/cholesky | solution.py:66
  422.2 9.8 %custom-call.8 = f32[1,128,128]{1,2,0:T(8,128)S(1)} custom-call(f32[1,128,128]{2,1,0:T(8,128)S(1)} %fusion.29), custom_call_target="InvertDiagBlocksLowerTriangular" | custom-call | tf_op jit(solution)/shard_map/triangular_solve | solution.py:68
  (142 shorter events, 129.1 us)
Async XLA Ops:
  19.6 5.2 %copy-start.6 = (s32[16,1440]{1,0:T(8,128)S(1)}, s32[16,1440]{1,0:T(8,128)}, u32[]{:S(2)}) copy-start(s32[16,1440]{1,0:T(8,128)} %param.17) | copy-start | bytes 276484
  19.6 5.3 %copy-start.4 = (f32[2,4,16,1440]{3,2,1,0:T(8,128)S(1)}, f32[2,4,16,1440]{3,2,1,0:T(8,128)}, u32[]{:S(2)}) copy-start(f32[2,4,16,1440]{3,2,1,0:T(8,128)} %param.16) | copy-start | bytes 2211844
  39.1 7.2 %copy-start = (f32[24,4,16,1440]{3,0,1,2:T(8,128)}, f32[24,4,16,1440]{3,0,1,2:T(8,128)S(1)}, u32[]{:S(2)}) copy-start(f32[24,4,16,1440]{3,0,1,2:T(8,128)S(1)} %get-tuple-element.102) | copy-start | bytes 26542084
  39.1 9.3 %copy-start.1 = (f32[24,4,16,1440]{3,0,1,2:T(8,128)}, f32[24,4,16,1440]{3,0,1,2:T(8,128)S(1)}, u32[]{:S(2)}) copy-start(f32[24,4,16,1440]{3,0,1,2:T(8,128)S(1)} %get-tuple-element.101) | copy-start | bytes 26542084
  117.9 8.2 %copy-start.3 = (f32[16,24,256]{2,1,0:T(8,128)S(1)}, f32[16,24,256]{2,1,0:T(8,128)}, u32[]{:S(2)}) copy-start(f32[16,24,256]{2,1,0:T(8,128)} %param.22) | copy-start | bytes 1179652
  117.9 10.0 %copy-start.7 = (f32[1,6,128]{2,0,1:T(1,128)S(1)}, f32[1,6,128]{2,0,1:T(1,128)}, u32[]{:S(2)}) copy-start(f32[1,6,128]{2,0,1:T(1,128)} %param.25) | copy-start | bytes 9220
  117.9 10.0 %copy-start.8 = (f32[1,6,128]{2,0,1:T(1,128)S(1)}, f32[1,6,128]{2,0,1:T(1,128)}, u32[]{:S(2)}) copy-start(f32[1,6,128]{2,0,1:T(1,128)} %param.26) | copy-start | bytes 9220
  117.9 79.0 %all-to-all-start = ((bf16[24,4,16,1440]{3,0,1,2:T(8,128)(2,1)}), bf16[24,4,16,1440]{3,0,1,2:T(8,128)(2,1)}, u32[]{:S(2)}, u32[]{:S(2)}) async-start(bf16[24,4,16,1440]{3,0,1,2:T(8,128)(2,1)} %fusion.22), calls=%async_computation | async-start | bytes 9437184 | tf_op jit(solution)/shard_map/all_to_all | solution.py:103
  126.1 306.5 %all-gather.2.cloned.1.call-start = ((), (), s32[]{:S(2)}) async-start(), calls=%async_computation.1 | async-start | bytes 3538944 | tf_op jit(solution)/shard_map/all_gather | solution.py:97
  127.1 85.4 %copy-start.9 = (bf16[256,256]{1,0:T(8,128)(2,1)S(1)}, bf16[256,256]{1,0:T(8,128)(2,1)}, u32[]{:S(2)}) copy-start(bf16[256,256]{1,0:T(8,128)(2,1)} %param.20) | copy-start | bytes 393220
  127.1 85.4 %copy-start.10 = (bf16[24,256]{1,0:T(8,128)(2,1)S(1)}, bf16[24,256]{1,0:T(8,128)(2,1)}, u32[]{:S(2)}) copy-start(bf16[24,256]{1,0:T(8,128)(2,1)} %param.18) | copy-start | bytes 36868
  127.1 85.4 %copy-start.11 = (f32[256]{0:T(256)S(1)}, f32[256]{0:T(256)}, u32[]{:S(2)}) copy-start(f32[256]{0:T(256)} %param.19) | copy-start | bytes 3076
  127.1 85.3 %copy-start.12 = (f32[256]{0:T(256)S(1)}, f32[256]{0:T(256)}, u32[]{:S(2)}) copy-start(f32[256]{0:T(256)} %param.21) | copy-start | bytes 3076
  212.5 140.8 %copy-start.13 = (s32[1,128]{1,0:T(1,128)S(1)}, s32[1,128]{1,0:T(1,128)}, u32[]{:S(2)}) copy-start(s32[1,128]{1,0:T(1,128)} %param.23) | copy-start | bytes 1540
  212.5 155.5 %copy-start.5 = (f32[128,1,6,128]{3,1,2,0:T(1,128)S(1)}, f32[128,1,6,128]{3,1,2,0:T(1,128)}, u32[]{:S(2)}) copy-start(f32[128,1,6,128]{3,1,2,0:T(1,128)} %param.27) | copy-start | bytes 1179652
  370.7 5.8 %collective-permute-start = (f32[2,128,128]{2,1,0:T(8,128)S(1)}, f32[2,128,128]{2,1,0:T(8,128)S(1)}, u32[]{:S(2)}, u32[]{:S(2)}) collective-permute-start(f32[2,128,128]{2,1,0:T(8,128)S(1)} %pad_maximum_fusion), channel_id=1, source_target_pairs={{0,1},{1,0},{2,3},{3,2},{4,5},{5,4},{6,7},{7,6},{8,9},{9,8},{10,11... | collective-permute-start | bytes 393224 | tf_op jit(solution)/shard_map/ppermute | solution.py:46
  376.6 6.6 %collective-permute-start.1 = (f32[2,128,128]{2,1,0:T(8,128)S(1)}, f32[2,128,128]{2,1,0:T(8,128)S(1)}, u32[]{:S(2)}, u32[]{:S(2)}) collective-permute-start(f32[2,128,128]{2,1,0:T(8,128)S(1)} %fusion.38), channel_id=1, source_target_pairs={{0,2},{1,3},{2,0},{3,1},{4,6},{5,7},{6,4},{7,5},{8,10},{9,11},{10,... | collective-permute-start | bytes 393224 | tf_op jit(solution)/shard_map/ppermute | solution.py:46
  383.1 5.0 %collective-permute-start.2 = (f32[2,128,128]{2,1,0:T(8,128)S(1)}, f32[2,128,128]{2,1,0:T(8,128)S(1)}, u32[]{:S(2)}, u32[]{:S(2)}) collective-permute-start(f32[2,128,128]{2,1,0:T(8,128)S(1)} %fusion.47), channel_id=1, source_target_pairs={{0,4},{1,5},{2,6},{3,7},{4,0},{5,1},{6,2},{7,3},{8,12},{9,13},{10,... | collective-permute-start | bytes 393224 | tf_op jit(solution)/shard_map/ppermute | solution.py:46
  388.2 20.8 %collective-permute-start.3 = (f32[2,128,128]{2,1,0:T(8,128)S(1)}, f32[2,128,128]{2,1,0:T(8,128)S(1)}, u32[]{:S(2)}, u32[]{:S(2)}) collective-permute-start(f32[2,128,128]{2,1,0:T(8,128)S(1)} %add.113), channel_id=1, source_target_pairs={{0,8},{1,9},{2,10},{3,11},{4,12},{5,13},{6,14},{7,15},{8,0},{9,1},... | collective-permute-start | bytes 393224 | tf_op jit(solution)/shard_map/ppermute | solution.py:46
  389.7 42.9 %copy-start.2 = (f32[2,8,24,256]{3,1,2,0:T(8,128)S(1)}, f32[2,8,24,256]{3,1,2,0:T(8,128)}, u32[]{:S(2)}) copy-start(f32[2,8,24,256]{3,1,2,0:T(8,128)} %copy.84) | copy-start | bytes 1179652
Sparse Core Ops, SparseCore 0:
  129.2 29.3 all-gather.1
